TPU v7x, 256 devices: a whole 4x4x8 slice. The times are simulated.
256 devices in a mesh: lon: 32 (over x_hi, z, core), lat: 8 (over x_lo, y).
Axes of the slice: x: 4 (x_hi: 2, x_lo: 2; x = x_hi * 2 + x_lo), y: 4, z: 8, core: 2. Of those that a mesh axis runs over, the one named last changes fastest.
Arguments:
- tracer_start: float32 [3, 16, 128, 4096], P(None, None, 'lat', 'lon'), may hold values from -6 to 6
- source: float32 [3, 16, 128, 4096], P(None, None, 'lat', 'lon'), may hold values from -3 to 3
- target: float32 [3, 16, 128, 4096], P(None, None, 'lat', 'lon'), may hold values from -27 to 27
- east_vel: float32 [16, 128, 4096], P(None, 'lat', 'lon'), may hold values from -0.12 to 0.12
- north_vel: float32 [16, 128, 4096], P(None, 'lat', 'lon'), may hold values from -0.12 to 0.12
- vertical_vel: float32 [16, 128, 4096], P(None, 'lat', 'lon'), may hold values from -0.12 to 0.12
- diffusivity: float32 [16, 128, 4096], P(None, 'lat', 'lon'), may hold values from 0.01 to 0.04
- sea_mask: int32 [16, 128, 4096], P(None, 'lat', 'lon'), may hold values 0 or 1
- reaction_rate: float32 [3, 16], replicated, may hold values from 0.05 to 0.5
- fold_partner: int32 [4096], P('lon'), may hold values from 0 to 4095, as said below
Outputs:
- source_grad: float32 [3, 16, 128, 4096], P(None, None, 'lat', 'lon')
- grad_norm: float32 [], replicated
Inputs may be any that keep to these rules, and one draw needn't show every extreme that they name: fold_partner[fold_partner[i]] = i; column i meets column (s - i) mod 4096 across the fold, for one s of each draw.
All inputs are finite; a program needn't handle non-finite values. No bound on the sum of `sea_mask` on one device may be relied on, other than what follows from the above.
Results may differ from a plain program's by a relative error of at most 0.00002.
Values sent between devices are 32-bit elements; how exact they have to be, the bound alone decides.
No kernel may reach another device: no remote copies, remote signals or barrier semaphores. Data moves between devices by JAX's collectives and lax.ppermute only.
A program may use at most 64 MiB of HBM per device.

v0:
```python
import jax
import jax.numpy as jnp
from jax import lax
from jax.sharding import PartitionSpec as P

STEPS = 4


def with_halo(block, sides, width, periodic):
    for axis, dim in sides:
        count = lax.axis_size(axis)
        forward = [(i, i + 1) for i in range(count - 1)]
        if periodic:
            forward.append((count - 1, 0))
        backward = [(target, source) for source, target in forward]
        low = lax.ppermute(
            lax.slice_in_dim(block, block.shape[dim] - width, None, axis=dim), axis, forward
        )
        high = lax.ppermute(lax.slice_in_dim(block, 0, width, axis=dim), axis, backward)
        block = jnp.concatenate([low, block, high], axis=dim)
    return block


def upwind_pair(velocity, mixing, face_sea):
    flow_rate = velocity * face_sea
    mixing_part = mixing * face_sea
    return (jnp.maximum(flow_rate, 0.0) + mixing_part, jnp.minimum(flow_rate, 0.0) - mixing_part)


def on_device(
    tracer_start,
    source,
    target,
    east_vel,
    north_vel,
    vertical_vel,
    diffusivity,
    sea_mask,
    reaction_rate,
    fold_partner,
):
    ocean = sea_mask.astype(jnp.float32)
    statics = jnp.stack([east_vel, north_vel, diffusivity, ocean])
    wide_static = with_halo(statics, (("lon", 3),), 1, True)
    tall_static = with_halo(statics, (("lat", 2),), 1, False)
    west_cell = wide_static[..., :-1]
    east_cell = wide_static[..., 1:]
    east_own, east_next = upwind_pair(
        west_cell[0], 0.5 * (west_cell[2] + east_cell[2]), west_cell[3] * east_cell[3]
    )
    below_row = tall_static[:, :, :-1, :]
    above_row = tall_static[:, :, 1:, :]
    north_own, north_next = upwind_pair(
        below_row[1], 0.5 * (below_row[2] + above_row[2]), below_row[3] * above_row[3]
    )
    up_own, up_next = upwind_pair(
        vertical_vel[:-1], 0.5 * (diffusivity[:-1] + diffusivity[1:]), ocean[:-1] * ocean[1:]
    )
    top_static = jnp.stack([north_vel[:, -1, :], diffusivity[:, -1, :], ocean[:, -1, :]])
    fold_all = lax.all_gather(top_static, "lon", axis=2, tiled=True)
    across = jnp.take(fold_all, fold_partner, axis=2)
    north_top = (lax.axis_index("lat") == lax.axis_size("lat") - 1).astype(jnp.float32)
    fold_own, fold_next = upwind_pair(
        0.5 * (top_static[0] - across[0]),
        0.5 * (top_static[1] + across[1]),
        top_static[2] * across[2] * north_top,
    )
    decay_rate = reaction_rate[:, :, None, None]

    def neighbours(quantity):
        east_west = with_halo(quantity, (("lon", 3),), 1, True)
        south_north = with_halo(quantity, (("lat", 2),), 1, False)
        top_row = quantity[:, :, -1, :]
        whole_top = lax.all_gather(top_row, "lon", axis=2, tiled=True)
        partner_row = jnp.take(whole_top, fold_partner, axis=2)
        return (east_west, south_north, partner_row)

    kept_states = [tracer_start]
    for repeat in range(STEPS):
        advance_quantity = kept_states[-1]
        uptake = decay_rate * advance_quantity / jnp.sqrt(1.0 + advance_quantity * advance_quantity)
        divergence_east_west, divergence_south_north, divergence_partner_row = neighbours(
            advance_quantity
        )
        east_flux = (
            east_own * divergence_east_west[..., :-1] + east_next * divergence_east_west[..., 1:]
        )
        north_flux = (
            north_own * divergence_south_north[:, :, :-1, :]
            + north_next * divergence_south_north[:, :, 1:, :]
        )
        divergence_top_row = advance_quantity[:, :, -1, :]
        fold_flux = fold_own * divergence_top_row + fold_next * divergence_partner_row
        north_flux = north_flux.at[:, :, -1, :].add(fold_flux)
        up_flux = up_own * advance_quantity[:, :-1] + up_next * advance_quantity[:, 1:]
        zero_level = jnp.zeros_like(advance_quantity[:, :1])
        vertical_part = jnp.concatenate([up_flux, zero_level], 1) - jnp.concatenate(
            [zero_level, up_flux], 1
        )
        kept_states.append(
            ocean
            * (
                advance_quantity
                - (
                    east_flux[..., 1:]
                    - east_flux[..., :-1]
                    + (north_flux[:, :, 1:, :] - north_flux[:, :, :-1, :])
                    + vertical_part
                )
                - uptake
                + source
            )
        )
    last_state = kept_states[-1]
    adjoint = ocean * (last_state - target)
    source_grad = ocean * adjoint
    for backward in range(STEPS - 1, 0, -1):
        current = kept_states[backward]
        weight = ocean * adjoint
        transposed_east_west, transposed_south_north, transposed_partner_row = neighbours(weight)
        east_diff = transposed_east_west[..., :-1] - transposed_east_west[..., 1:]
        north_diff = transposed_south_north[:, :, :-1, :] - transposed_south_north[:, :, 1:, :]
        up_diff = weight[:, :-1] - weight[:, 1:]
        result = east_own[..., 1:] * east_diff[..., 1:] + east_next[..., :-1] * east_diff[..., :-1]
        result = result + (
            north_own[:, 1:, :] * north_diff[:, :, 1:, :]
            + north_next[:, :-1, :] * north_diff[:, :, :-1, :]
        )
        result = result.at[:, :, -1, :].add(
            fold_own * (weight[:, :, -1, :] - transposed_partner_row)
        )
        transposed_zero_level = jnp.zeros_like(weight[:, :1])
        result = result + (
            jnp.concatenate([up_own * up_diff, transposed_zero_level], 1)
            + jnp.concatenate([transposed_zero_level, up_next * up_diff], 1)
        )
        spread = 1.0 + current * current
        adjoint = weight - result - decay_rate / (spread * jnp.sqrt(spread)) * weight
        source_grad = source_grad + ocean * adjoint
    squares = lax.psum(jnp.sum(source_grad * source_grad), ("lon", "lat"))
    return (source_grad, jnp.sqrt(squares))


def solution(mesh):
    return jax.shard_map(
        on_device,
        mesh=mesh,
        in_specs=(
            P(None, None, "lat", "lon"),
            P(None, None, "lat", "lon"),
            P(None, None, "lat", "lon"),
            P(None, "lat", "lon"),
            P(None, "lat", "lon"),
            P(None, "lat", "lon"),
            P(None, "lat", "lon"),
            P(None, "lat", "lon"),
            P(),
            P("lon"),
        ),
        out_specs=(P(None, None, "lat", "lon"), P()),
        check_vma=False,
    )
```

profile of v0, /device:TPU:1, one launch (start us, length us, event | category | flops | bytes accessed | tf_op | source)
XLA Modules:
  0.0 698.3 jit_solution(13284979570440464098)
XLA Ops:
  3.1 4.6 collective-permute-start.6
  23.0 48.5 %all-gather = f32[3,16,1,4096]{3,1,2,0:T(8,128)} all-gather(f32[3,16,1,128]{3,1,2,0:T(8,128)S(1)} %get-tuple-element.158), channel_id=2, replica_groups=mesh['lon'=32,'lat'=8] {'lon'}, dimensions={3}, use_global_device_ids=true | all-gather | bytes 811008 | tf_op jit(solution)/shard_map/all_gather | solution.py:74
  71.5 39.1 %all_gather.24 = f32[3,16,4096]{2,1,0:T(8,128)S(1)} all-gather(f32[3,16,128]{2,1,0:T(8,128)S(1)} %pad_maximum_fusion.12), channel_id=1, replica_groups=mesh['lon'=32,'lat'=8] {'lon'}, dimensions={2}, use_global_device_ids=true | all-gather | bytes 811008 | tf_op jit(solution)/shard_map/all_gather | solution.py:60
  110.6 5.8 copy.549
  116.5 4.2 gather_fusion
  122.8 6.9 copy.552
  129.7 4.1 gather_fusion.1
  140.8 4.7 collective-permute-start.4
  164.8 49.4 %all-gather.1 = f32[3,16,1,4096]{3,1,2,0:T(8,128)} all-gather(f32[3,16,1,128]{3,1,2,0:T(8,128)S(1)} %get-tuple-element.153), channel_id=3, replica_groups=mesh['lon'=32,'lat'=8] {'lon'}, dimensions={3}, use_global_device_ids=true | all-gather | bytes 811008 | tf_op jit(solution)/shard_map/all_gather | solution.py:74
  214.2 6.8 copy.567
  221.1 4.3 gather_fusion.2
  233.6 4.3 collective-permute-start.14
  239.8 50.3 %all-gather.2 = f32[3,16,1,4096]{3,1,2,0:T(8,128)} all-gather(f32[3,16,1,128]{3,1,2,0:T(8,128)S(1)} %get-tuple-element.148), channel_id=4, replica_groups=mesh['lon'=32,'lat'=8] {'lon'}, dimensions={3}, use_global_device_ids=true | all-gather | bytes 811008 | tf_op jit(solution)/shard_map/all_gather | solution.py:74
  290.1 6.8 copy.585
  296.9 4.9 gather_fusion.3
  311.2 4.3 collective-permute-start.18
  317.4 50.3 %all-gather.3 = f32[3,16,1,4096]{3,1,2,0:T(8,128)} all-gather(f32[3,16,1,128]{3,1,2,0:T(8,128)S(1)} %get-tuple-element.143), channel_id=5, replica_groups=mesh['lon'=32,'lat'=8] {'lon'}, dimensions={3}, use_global_device_ids=true | all-gather | bytes 811008 | tf_op jit(solution)/shard_map/all_gather | solution.py:74
  367.7 6.8 copy.597
  374.5 4.9 gather_fusion.4
  388.3 6.1 collective-permute-start.22
  396.5 50.1 %all-gather.4 = f32[3,16,1,4096]{3,1,2,0:T(8,128)} all-gather(f32[3,16,1,128]{3,1,2,0:T(8,128)S(1)} %get-tuple-element.137), channel_id=6, replica_groups=mesh['lon'=32,'lat'=8] {'lon'}, dimensions={3}, use_global_device_ids=true | all-gather | bytes 811008 | tf_op jit(solution)/shard_map/all_gather | solution.py:74
  446.6 6.9 copy.618
  453.5 4.9 gather_fusion.5
  465.2 6.4 collective-permute-start.26
  473.5 50.1 %all-gather.5 = f32[3,16,1,4096]{3,1,2,0:T(8,128)} all-gather(f32[3,16,1,128]{3,1,2,0:T(8,128)S(1)} %get-tuple-element.130), channel_id=7, replica_groups=mesh['lon'=32,'lat'=8] {'lon'}, dimensions={3}, use_global_device_ids=true | all-gather | bytes 811008 | tf_op jit(solution)/shard_map/all_gather | solution.py:74
  523.5 6.8 copy.631
  530.4 4.9 gather_fusion.6
  541.6 6.4 collective-permute-start.30
  549.9 47.6 %all-gather.6 = f32[3,16,1,4096]{3,1,2,0:T(8,128)S(1)} all-gather(f32[3,16,1,128]{3,1,2,0:T(8,128)S(1)} %get-tuple-element.120), channel_id=8, replica_groups=mesh['lon'=32,'lat'=8] {'lon'}, dimensions={3}, use_global_device_ids=true | all-gather | bytes 811008 | tf_op jit(solution)/shard_map/all_gather | solution.py:74
  597.6 5.8 copy.645
  603.4 4.3 gather_fusion.7
  612.6 83.9 %psum.7 = f32[]{:T(128)} all-reduce(f32[]{:T(128)} %get-tuple-element.93), channel_id=1, replica_groups=mesh['lon'=32,'lat'=8] {'lon','lat'}, use_global_device_ids=true, to_apply=%region_1.3 | all-reduce | flops 1 | bytes 8 | tf_op jit(solution)/shard_map/psum | solution.py:140
  (203 shorter events, 99.6 us)
Async XLA Ops:
  3.1 144.9 %collective-permute-start.6 = (f32[3,16,1,128]{3,1,0,2:T(8,128)}, f32[3,16,1,128]{3,1,0,2:T(8,128)}, u32[]{:S(2)}, u32[]{:S(2)}) collective-permute-start(f32[3,16,1,128]{3,1,0,2:T(8,128)} %get-tuple-element.160), channel_id=1, source_target_pairs={{0,1},{1,2},{2,3},{3,4},{4,5},{5,6},{6,7},{8,9},{9,10},{10,11},{11... | collective-permute-start | bytes 73736 | tf_op jit(solution)/shard_map/ppermute | solution.py:16
  7.8 140.3 %collective-permute-start.7 = (f32[3,16,1,128]{3,1,0,2:T(8,128)}, f32[3,16,1,128]{3,1,0,2:T(8,128)}, u32[]{:S(2)}, u32[]{:S(2)}) collective-permute-start(f32[3,16,1,128]{3,1,0,2:T(8,128)} %get-tuple-element.159), channel_id=1, source_target_pairs={{1,0},{2,1},{3,2},{4,3},{5,4},{6,5},{7,6},{9,8},{10,9},{11,10},{12... | collective-permute-start | bytes 73736 | tf_op jit(solution)/shard_map/ppermute | solution.py:19
  11.8 134.2 %collective-permute-start.5 = (f32[4,16,1,128]{3,2,1,0:T(1,128)}, f32[4,16,1,128]{3,2,1,0:T(1,128)}, u32[]{:S(2)}, u32[]{:S(2)}) collective-permute-start(f32[4,16,1,128]{3,2,1,0:T(1,128)} %get-tuple-element.119), channel_id=1, source_target_pairs={{1,0},{2,1},{3,2},{4,3},{5,4},{6,5},{7,6},{9,8},{10,9},{11,10},{12... | collective-permute-start | bytes 98312 | tf_op jit(solution)/shard_map/ppermute | solution.py:19
  14.2 120.3 %collective-permute-start.1 = (f32[4,16,16,1]{3,2,1,0:T(8,128)}, f32[4,16,16,1]{3,2,1,0:T(8,128)}, u32[]{:S(2)}, u32[]{:S(2)}) collective-permute-start(f32[4,16,16,1]{3,2,1,0:T(8,128)} %get-tuple-element.117), channel_id=1, source_target_pairs={{8,0},{16,8},{24,16},{32,24},{40,32},{48,40},{56,48},{64,56},{72,6... | collective-permute-start | bytes 12296 | tf_op jit(solution)/shard_map/ppermute | solution.py:19
  15.2 120.6 %collective-permute-start = (f32[4,16,16,1]{3,2,1,0:T(8,128)}, f32[4,16,16,1]{3,2,1,0:T(8,128)}, u32[]{:S(2)}, u32[]{:S(2)}) collective-permute-start(f32[4,16,16,1]{3,2,1,0:T(8,128)} %get-tuple-element.116), channel_id=1, source_target_pairs={{0,8},{8,16},{16,24},{24,32},{32,40},{40,48},{48,56},{56,64},{64,7... | collective-permute-start | bytes 12296 | tf_op jit(solution)/shard_map/ppermute | solution.py:16
  134.5 6.3 collective-permute-start.2
  135.8 9.7 %collective-permute-start.3 = (f32[3,16,16,1]{3,2,1,0:T(8,128)}, f32[3,16,16,1]{3,2,1,0:T(8,128)S(1)}, u32[]{:S(2)}, u32[]{:S(2)}) collective-permute-start(f32[3,16,16,1]{3,2,1,0:T(8,128)} %get-tuple-element.156), channel_id=1, source_target_pairs={{8,0},{16,8},{24,16},{32,24},{40,32},{48,40},{56,48},{64,56},{72,6... | collective-permute-start | bytes 9224 | tf_op jit(solution)/shard_map/ppermute | solution.py:19
  140.8 6.0 collective-permute-start.4
  152.6 75.1 %collective-permute-start.10 = (f32[3,16,1,128]{3,1,0,2:T(8,128)S(1)}, f32[3,16,1,128]{3,1,0,2:T(8,128)S(1)}, u32[]{:S(2)}, u32[]{:S(2)}) collective-permute-start(f32[3,16,1,128]{3,1,0,2:T(8,128)S(1)} %get-tuple-element.155), channel_id=1, source_target_pairs={{0,1},{1,2},{2,3},{3,4},{4,5},{5,6},{6,7},{8,9},{9,10},{10,11},{11... | collective-permute-start | bytes 73736 | tf_op jit(solution)/shard_map/ppermute | solution.py:16
  156.3 71.5 %collective-permute-start.11 = (f32[3,16,1,128]{3,1,0,2:T(8,128)S(1)}, f32[3,16,1,128]{3,1,0,2:T(8,128)S(1)}, u32[]{:S(2)}, u32[]{:S(2)}) collective-permute-start(f32[3,16,1,128]{3,1,0,2:T(8,128)S(1)} %get-tuple-element.154), channel_id=1, source_target_pairs={{1,0},{2,1},{3,2},{4,3},{5,4},{6,5},{7,6},{9,8},{10,9},{11,10},{12... | collective-permute-start | bytes 73736 | tf_op jit(solution)/shard_map/ppermute | solution.py:19
  157.6 68.6 %collective-permute-start.8 = (f32[3,16,16,1]{3,2,1,0:T(8,128)}, f32[3,16,16,1]{3,2,1,0:T(8,128)}, u32[]{:S(2)}, u32[]{:S(2)}) collective-permute-start(f32[3,16,16,1]{3,2,1,0:T(8,128)} %get-tuple-element.152), channel_id=1, source_target_pairs={{0,8},{8,16},{16,24},{24,32},{32,40},{40,48},{48,56},{56,64},{64,7... | collective-permute-start | bytes 9224 | tf_op jit(solution)/shard_map/ppermute | solution.py:16
  161.3 64.8 %collective-permute-start.9 = (f32[3,16,16,1]{3,2,1,0:T(8,128)}, f32[3,16,16,1]{3,2,1,0:T(8,128)}, u32[]{:S(2)}, u32[]{:S(2)}) collective-permute-start(f32[3,16,16,1]{3,2,1,0:T(8,128)} %get-tuple-element.151), channel_id=1, source_target_pairs={{8,0},{16,8},{24,16},{32,24},{40,32},{48,40},{56,48},{64,56},{72,6... | collective-permute-start | bytes 9224 | tf_op jit(solution)/shard_map/ppermute | solution.py:19
  233.6 72.0 %collective-permute-start.14 = (f32[3,16,1,128]{3,1,0,2:T(8,128)S(1)}, f32[3,16,1,128]{3,1,0,2:T(8,128)S(1)}, u32[]{:S(2)}, u32[]{:S(2)}) collective-permute-start(f32[3,16,1,128]{3,1,0,2:T(8,128)S(1)} %get-tuple-element.150), channel_id=1, source_target_pairs={{0,1},{1,2},{2,3},{3,4},{4,5},{5,6},{6,7},{8,9},{9,10},{10,11},{11... | collective-permute-start | bytes 73736 | tf_op jit(solution)/shard_map/ppermute | solution.py:16
  237.9 67.8 %collective-permute-start.15 = (f32[3,16,1,128]{3,1,0,2:T(8,128)S(1)}, f32[3,16,1,128]{3,1,0,2:T(8,128)S(1)}, u32[]{:S(2)}, u32[]{:S(2)}) collective-permute-start(f32[3,16,1,128]{3,1,0,2:T(8,128)S(1)} %get-tuple-element.149), channel_id=1, source_target_pairs={{1,0},{2,1},{3,2},{4,3},{5,4},{6,5},{7,6},{9,8},{10,9},{11,10},{12... | collective-permute-start | bytes 73736 | tf_op jit(solution)/shard_map/ppermute | solution.py:19
  239.2 63.7 %collective-permute-start.12 = (f32[3,16,16,1]{3,1,0,2:T(8,128)}, f32[3,16,16,1]{3,1,0,2:T(8,128)}, u32[]{:S(2)}, u32[]{:S(2)}) collective-permute-start(f32[3,16,16,1]{3,1,0,2:T(8,128)} %get-tuple-element.147), channel_id=1, source_target_pairs={{0,8},{8,16},{16,24},{24,32},{32,40},{40,48},{48,56},{56,64},{64,7... | collective-permute-start | bytes 9224 | tf_op jit(solution)/shard_map/ppermute | solution.py:16
  239.3 64.8 %collective-permute-start.13 = (f32[3,16,16,1]{3,1,0,2:T(8,128)}, f32[3,16,16,1]{3,1,0,2:T(8,128)}, u32[]{:S(2)}, u32[]{:S(2)}) collective-permute-start(f32[3,16,16,1]{3,1,0,2:T(8,128)} %get-tuple-element.146), channel_id=1, source_target_pairs={{8,0},{16,8},{24,16},{32,24},{40,32},{48,40},{56,48},{64,56},{72,6... | collective-permute-start | bytes 9224 | tf_op jit(solution)/shard_map/ppermute | solution.py:19
  311.2 73.1 %collective-permute-start.18 = (f32[3,16,1,128]{3,1,0,2:T(8,128)S(1)}, f32[3,16,1,128]{3,1,0,2:T(8,128)S(1)}, u32[]{:S(2)}, u32[]{:S(2)}) collective-permute-start(f32[3,16,1,128]{3,1,0,2:T(8,128)S(1)} %get-tuple-element.145), channel_id=1, source_target_pairs={{0,1},{1,2},{2,3},{3,4},{4,5},{5,6},{6,7},{8,9},{9,10},{10,11},{11... | collective-permute-start | bytes 73736 | tf_op jit(solution)/shard_map/ppermute | solution.py:16
  315.5 68.9 %collective-permute-start.19 = (f32[3,16,1,128]{3,1,0,2:T(8,128)S(1)}, f32[3,16,1,128]{3,1,0,2:T(8,128)S(1)}, u32[]{:S(2)}, u32[]{:S(2)}) collective-permute-start(f32[3,16,1,128]{3,1,0,2:T(8,128)S(1)} %get-tuple-element.144), channel_id=1, source_target_pairs={{1,0},{2,1},{3,2},{4,3},{5,4},{6,5},{7,6},{9,8},{10,9},{11,10},{12... | collective-permute-start | bytes 73736 | tf_op jit(solution)/shard_map/ppermute | solution.py:19
  316.8 63.7 %collective-permute-start.16 = (f32[3,16,16,1]{3,1,0,2:T(8,128)}, f32[3,16,16,1]{3,1,0,2:T(8,128)}, u32[]{:S(2)}, u32[]{:S(2)}) collective-permute-start(f32[3,16,16,1]{3,1,0,2:T(8,128)} %get-tuple-element.142), channel_id=1, source_target_pairs={{0,8},{8,16},{16,24},{24,32},{32,40},{40,48},{48,56},{56,64},{64,7... | collective-permute-start | bytes 9224 | tf_op jit(solution)/shard_map/ppermute | solution.py:16
  316.9 64.8 %collective-permute-start.17 = (f32[3,16,16,1]{3,1,0,2:T(8,128)}, f32[3,16,16,1]{3,1,0,2:T(8,128)}, u32[]{:S(2)}, u32[]{:S(2)}) collective-permute-start(f32[3,16,16,1]{3,1,0,2:T(8,128)} %get-tuple-element.141), channel_id=1, source_target_pairs={{8,0},{16,8},{24,16},{32,24},{40,32},{48,40},{56,48},{64,56},{72,6... | collective-permute-start | bytes 9224 | tf_op jit(solution)/shard_map/ppermute | solution.py:19
  388.3 72.8 %collective-permute-start.22 = (f32[3,16,1,128]{3,1,0,2:T(8,128)S(1)}, f32[3,16,1,128]{3,1,0,2:T(8,128)S(1)}, u32[]{:S(2)}, u32[]{:S(2)}) collective-permute-start(f32[3,16,1,128]{3,1,0,2:T(8,128)S(1)} %get-tuple-element.138), channel_id=1, source_target_pairs={{0,1},{1,2},{2,3},{3,4},{4,5},{5,6},{6,7},{8,9},{9,10},{10,11},{11... | collective-permute-start | bytes 73736 | tf_op jit(solution)/shard_map/ppermute | solution.py:16
  394.4 66.7 %collective-permute-start.23 = (f32[3,16,1,128]{3,2,1,0:T(1,128)S(1)}, f32[3,16,1,128]{3,2,1,0:T(1,128)}, u32[]{:S(2)}, u32[]{:S(2)}) collective-permute-start(f32[3,16,1,128]{3,2,1,0:T(1,128)S(1)} %slice.756), channel_id=1, source_target_pairs={{1,0},{2,1},{3,2},{4,3},{5,4},{6,5},{7,6},{9,8},{10,9},{11,10},{12... | collective-permute-start | bytes 73736 | tf_op jit(solution)/shard_map/ppermute | solution.py:19
  395.7 63.8 %collective-permute-start.20 = (f32[3,16,16,1]{3,1,0,2:T(8,128)}, f32[3,16,16,1]{3,1,0,2:T(8,128)}, u32[]{:S(2)}, u32[]{:S(2)}) collective-permute-start(f32[3,16,16,1]{3,1,0,2:T(8,128)} %get-tuple-element.140), channel_id=1, source_target_pairs={{0,8},{8,16},{16,24},{24,32},{32,40},{40,48},{48,56},{56,64},{64,7... | collective-permute-start | bytes 9224 | tf_op jit(solution)/shard_map/ppermute | solution.py:16
  396.0 63.5 %collective-permute-start.21 = (f32[3,16,16,1]{3,1,0,2:T(8,128)S(1)}, f32[3,16,16,1]{3,1,0,2:T(8,128)}, u32[]{:S(2)}, u32[]{:S(2)}) collective-permute-start(f32[3,16,16,1]{3,1,0,2:T(8,128)S(1)} %get-tuple-element.139), channel_id=1, source_target_pairs={{8,0},{16,8},{24,16},{32,24},{40,32},{48,40},{56,48},{64,56},{72,6... | collective-permute-start | bytes 9224 | tf_op jit(solution)/shard_map/ppermute | solution.py:19
  465.2 72.6 %collective-permute-start.26 = (f32[3,16,1,128]{3,1,0,2:T(8,128)S(1)}, f32[3,16,1,128]{3,1,0,2:T(8,128)S(1)}, u32[]{:S(2)}, u32[]{:S(2)}) collective-permute-start(f32[3,16,1,128]{3,1,0,2:T(8,128)S(1)} %get-tuple-element.131), channel_id=1, source_target_pairs={{0,1},{1,2},{2,3},{3,4},{4,5},{5,6},{6,7},{8,9},{9,10},{10,11},{11... | collective-permute-start | bytes 73736 | tf_op jit(solution)/shard_map/ppermute | solution.py:16
  471.5 66.2 %collective-permute-start.27 = (f32[3,16,1,128]{3,1,0,2:T(8,128)S(1)}, f32[3,16,1,128]{3,1,0,2:T(8,128)S(1)}, u32[]{:S(2)}, u32[]{:S(2)}) collective-permute-start(f32[3,16,1,128]{3,1,0,2:T(8,128)S(1)} %get-tuple-element.132), channel_id=1, source_target_pairs={{1,0},{2,1},{3,2},{4,3},{5,4},{6,5},{7,6},{9,8},{10,9},{11,10},{12... | collective-permute-start | bytes 73736 | tf_op jit(solution)/shard_map/ppermute | solution.py:19
  472.8 63.5 %collective-permute-start.24 = (f32[3,16,16,1]{3,1,0,2:T(8,128)S(1)}, f32[3,16,16,1]{3,1,0,2:T(8,128)}, u32[]{:S(2)}, u32[]{:S(2)}) collective-permute-start(f32[3,16,16,1]{3,1,0,2:T(8,128)S(1)} %get-tuple-element.134), channel_id=1, source_target_pairs={{0,8},{8,16},{16,24},{24,32},{32,40},{40,48},{48,56},{56,64},{64,7... | collective-permute-start | bytes 9224 | tf_op jit(solution)/shard_map/ppermute | solution.py:16
  472.9 63.4 %collective-permute-start.25 = (f32[3,16,16,1]{3,1,0,2:T(8,128)S(1)}, f32[3,16,16,1]{3,1,0,2:T(8,128)}, u32[]{:S(2)}, u32[]{:S(2)}) collective-permute-start(f32[3,16,16,1]{3,1,0,2:T(8,128)S(1)} %get-tuple-element.133), channel_id=1, source_target_pairs={{8,0},{16,8},{24,16},{32,24},{40,32},{48,40},{56,48},{64,56},{72,6... | collective-permute-start | bytes 9224 | tf_op jit(solution)/shard_map/ppermute | solution.py:19
  541.6 67.5 %collective-permute-start.30 = (f32[3,16,1,128]{3,1,0,2:T(8,128)S(1)}, f32[3,16,1,128]{3,1,0,2:T(8,128)S(1)}, u32[]{:S(2)}, u32[]{:S(2)}) collective-permute-start(f32[3,16,1,128]{3,1,0,2:T(8,128)S(1)} %get-tuple-element.121), channel_id=1, source_target_pairs={{0,1},{1,2},{2,3},{3,4},{4,5},{5,6},{6,7},{8,9},{9,10},{10,11},{11... | collective-permute-start | bytes 73736 | tf_op jit(solution)/shard_map/ppermute | solution.py:16
  548.0 61.2 %collective-permute-start.31 = (f32[3,16,1,128]{3,1,0,2:T(8,128)S(1)}, f32[3,16,1,128]{3,1,0,2:T(8,128)S(1)}, u32[]{:S(2)}, u32[]{:S(2)}) collective-permute-start(f32[3,16,1,128]{3,1,0,2:T(8,128)S(1)} %get-tuple-element.122), channel_id=1, source_target_pairs={{1,0},{2,1},{3,2},{4,3},{5,4},{6,5},{7,6},{9,8},{10,9},{11,10},{12... | collective-permute-start | bytes 73736 | tf_op jit(solution)/shard_map/ppermute | solution.py:19
  549.3 58.4 %collective-permute-start.28 = (f32[3,16,16,1]{3,1,0,2:T(8,128)}, f32[3,16,16,1]{3,1,0,2:T(8,128)}, u32[]{:S(2)}, u32[]{:S(2)}) collective-permute-start(f32[3,16,16,1]{3,1,0,2:T(8,128)} %get-tuple-element.124), channel_id=1, source_target_pairs={{0,8},{8,16},{16,24},{24,32},{32,40},{40,48},{48,56},{56,64},{64,7... | collective-permute-start | bytes 9224 | tf_op jit(solution)/shard_map/ppermute | solution.py:16
  549.4 58.4 %collective-permute-start.29 = (f32[3,16,16,1]{3,1,0,2:T(8,128)}, f32[3,16,16,1]{3,1,0,2:T(8,128)}, u32[]{:S(2)}, u32[]{:S(2)}) collective-permute-start(f32[3,16,16,1]{3,1,0,2:T(8,128)} %get-tuple-element.123), channel_id=1, source_target_pairs={{8,0},{16,8},{24,16},{32,24},{40,32},{48,40},{56,48},{64,56},{72,6... | collective-permute-start | bytes 9224 | tf_op jit(solution)/shard_map/ppermute | solution.py:19
  (17 other events, 827.8 us)
where the time goes:
time: 701 us; the launch traced here: 698 us
  blocking collectives  469 us (67%)
  local copies, waits for them, and re-layouts  115 us (16%)
  starting transfers between devices  63.9 us (9%)
  other arithmetic  42.6 us (6%)
    all_gather x7, blocking collectives, neighbours(): whole_top = lax.all_gather(top_row, 'lon', axis=2, tiled=True)  346 us
    psum x1, blocking collectives, on_device(): squares = lax.psum(jnp.sum(source_grad * source_grad), ('lon', 'lat'))  83.9 us
    ppermute x16, starting transfers between devices, with_halo(): lax.ppermute(lax.slice_in_dim(block, block.shape[dim] - width, None, axis...  47.4 us
    all_gather x7, local copies, waits for them, and re-layouts, neighbours(): whole_top = lax.all_gather(top_row, 'lon', axis=2, tiled=True)  46.9 us
    all_gather x1, blocking collectives, on_device(): fold_all = lax.all_gather(top_static, 'lon', axis=2, tiled=True)  39.1 us
    gather x14, local copies, waits for them, and re-layouts, neighbours(): partner_row = jnp.take(whole_top, fold_partner, axis=2)  37.4 us
    ppermute x16, starting transfers between devices, with_halo(): lax.ppermute(lax.slice_in_dim(block, 0, width, axis=dim), axis, backward)  16.5 us
  transfers between devices with their start and end apart: 32, of which 2 were waited for; matrix products, arithmetic and copies ran while one was open for 18% of the time, Pallas kernels for 0%

commit v1 on v0

--- a/solution.py
+++ b/solution.py
@@ -57,7 +57,9 @@
         vertical_vel[:-1], 0.5 * (diffusivity[:-1] + diffusivity[1:]), ocean[:-1] * ocean[1:]
     )
     top_static = jnp.stack([north_vel[:, -1, :], diffusivity[:, -1, :], ocean[:, -1, :]])
-    fold_all = lax.all_gather(top_static, "lon", axis=2, tiled=True)
+    fold_all = jnp.concatenate(
+        lax.all_to_all(jnp.stack([top_static] * lax.axis_size("lon")), "lon", 0, 0), axis=2
+    )
     across = jnp.take(fold_all, fold_partner, axis=2)
     north_top = (lax.axis_index("lat") == lax.axis_size("lat") - 1).astype(jnp.float32)
     fold_own, fold_next = upwind_pair(

time: 701 us -> 675 us (0.963)
  blocking collectives: 469 us -> 437 us
  starting transfers between devices: 63.9 us -> 73.3 us
    all_gather x1 -> x0, blocking collectives: 39.1 us -> none  [on_device(): fold_all = lax.all_gather(top_static, 'lon', axis=2, tiled=True)]
    all_to_all x0 -> x1, starting transfers between devices: none -> 12.1 us  [on_device(): lax.all_to_all(jnp.stack([top_static] * lax.axis_size('lon')), 'lon', 0, 0)]
  transfers between devices with their start and end apart: 32 -> 33, of which waited for: 2 -> 1; matrix products, arithmetic and copies ran while one was open for 18% -> 17% of each run, Pallas kernels for 0% -> 0%
where the time goes in v1:
time: 675 us; the launch traced here: 672 us
  blocking collectives  437 us (65%)
  local copies, waits for them, and re-layouts  114 us (17%)
  starting transfers between devices  73.3 us (11%)
  other arithmetic  40.6 us (6%)
    all_gather x7, blocking collectives, neighbours(): whole_top = lax.all_gather(top_row, 'lon', axis=2, tiled=True)  351 us
    psum x1, blocking collectives, on_device(): squares = lax.psum(jnp.sum(source_grad * source_grad), ('lon', 'lat'))  85.9 us
    ppermute x16, starting transfers between devices, with_halo(): lax.ppermute(lax.slice_in_dim(block, block.shape[dim] - width, None, axis...  45.7 us
    all_gather x7, local copies, waits for them, and re-layouts, neighbours(): whole_top = lax.all_gather(top_row, 'lon', axis=2, tiled=True)  45.6 us
    gather x14, local copies, waits for them, and re-layouts, neighbours(): partner_row = jnp.take(whole_top, fold_partner, axis=2)  37.1 us
    ppermute x16, starting transfers between devices, with_halo(): lax.ppermute(lax.slice_in_dim(block, 0, width, axis=dim), axis, backward)  15.5 us
  transfers between devices with their start and end apart: 33, of which 1 were waited for; matrix products, arithmetic and copies ran while one was open for 17% of the time, Pallas kernels for 0%

profile of v1, /device:TPU:1, one launch (start us, length us, event | category | flops | bytes accessed | tf_op | source)
XLA Modules:
  0.0 671.6 jit_solution(8440913600586480073)
XLA Ops:
  3.3 4.6 collective-permute-start.6
  15.9 12.1 %all-to-all-start = ((f32[32,3,16,128]{3,2,1,0:T(8,128)}), f32[32,3,16,128]{3,2,1,0:T(8,128)}, u32[]{:S(2)}, u32[]{:S(2)}) async-start(f32[32,3,16,128]{3,2,1,0:T(8,128)} %stack.17), calls=%async_computation | async-start | bytes 1572864 | tf_op jit(solution)/shard_map/all_to_all | solution.py:61
  33.0 55.3 %all-gather = f32[3,16,1,4096]{3,1,2,0:T(8,128)S(1)} all-gather(f32[3,16,1,128]{3,1,2,0:T(8,128)S(1)} %get-tuple-element.158), channel_id=2, replica_groups=mesh['lon'=32,'lat'=8] {'lon'}, dimensions={3}, use_global_device_ids=true | all-gather | bytes 811008 | tf_op jit(solution)/shard_map/all_gather | solution.py:76
  90.0 5.8 copy.558
  95.8 4.1 gather_fusion.1
  105.8 4.9 collective-permute-start.4
  116.1 6.8 %copy.657 = f32[3,16,32,128]{1,0,3,2:T(4,128)} copy(f32[3,16,32,128]{3,1,0,2:T(8,128)} %bitcast.13) | data formatting | bytes 1572864 | tf_op jit(solution)/shard_map/reshape | solution.py:60
  122.9 4.1 gather_fusion
  137.0 47.8 %all-gather.1 = f32[3,16,1,4096]{3,1,2,0:T(8,128)} all-gather(f32[3,16,1,128]{3,1,2,0:T(8,128)S(1)} %get-tuple-element.153), channel_id=3, replica_groups=mesh['lon'=32,'lat'=8] {'lon'}, dimensions={3}, use_global_device_ids=true | all-gather | bytes 811008 | tf_op jit(solution)/shard_map/all_gather | solution.py:76
  187.3 6.8 %copy.573 = f32[3,16,1,4096]{1,0,3,2:T(4,128)} copy(f32[3,16,1,4096]{3,1,2,0:T(8,128)} %all-gather.1) | data formatting | bytes 1572864 | tf_op jit(solution)/shard_map/all_gather | solution.py:76
  194.2 4.1 gather_fusion.2
  204.9 4.3 collective-permute-start.14
  214.7 50.3 %all-gather.2 = f32[3,16,1,4096]{3,1,2,0:T(8,128)} all-gather(f32[3,16,1,128]{3,1,2,0:T(8,128)S(1)} %get-tuple-element.148), channel_id=4, replica_groups=mesh['lon'=32,'lat'=8] {'lon'}, dimensions={3}, use_global_device_ids=true | all-gather | bytes 811008 | tf_op jit(solution)/shard_map/all_gather | solution.py:76
  265.0 6.8 %copy.591 = f32[3,16,1,4096]{1,0,3,2:T(4,128)} copy(f32[3,16,1,4096]{3,1,2,0:T(8,128)} %all-gather.2) | data formatting | bytes 1572864 | tf_op jit(solution)/shard_map/all_gather | solution.py:76
  271.8 4.8 gather_fusion.3
  285.1 4.9 collective-permute-start.18
  291.8 50.3 %all-gather.3 = f32[3,16,1,4096]{3,1,2,0:T(8,128)} all-gather(f32[3,16,1,128]{3,1,2,0:T(8,128)S(1)} %get-tuple-element.143), channel_id=5, replica_groups=mesh['lon'=32,'lat'=8] {'lon'}, dimensions={3}, use_global_device_ids=true | all-gather | bytes 811008 | tf_op jit(solution)/shard_map/all_gather | solution.py:76
  342.1 6.8 %copy.603 = f32[3,16,1,4096]{1,0,3,2:T(4,128)} copy(f32[3,16,1,4096]{3,1,2,0:T(8,128)} %all-gather.3) | data formatting | bytes 1572864 | tf_op jit(solution)/shard_map/all_gather | solution.py:76
  349.0 4.8 gather_fusion.4
  361.6 5.1 collective-permute-start.22
  368.8 49.9 %all-gather.4 = f32[3,16,1,4096]{3,1,2,0:T(8,128)} all-gather(f32[3,16,1,128]{3,1,2,0:T(8,128)S(1)} %get-tuple-element.137), channel_id=6, replica_groups=mesh['lon'=32,'lat'=8] {'lon'}, dimensions={3}, use_global_device_ids=true | all-gather | bytes 811008 | tf_op jit(solution)/shard_map/all_gather | solution.py:76
  418.7 6.8 %copy.624 = f32[3,16,1,4096]{1,0,3,2:T(4,128)} copy(f32[3,16,1,4096]{3,1,2,0:T(8,128)} %all-gather.4) | data formatting | bytes 1572864 | tf_op jit(solution)/shard_map/all_gather | solution.py:76
  425.4 4.9 gather_fusion.5
  436.6 6.4 collective-permute-start.26
  444.9 50.1 %all-gather.5 = f32[3,16,1,4096]{3,1,2,0:T(8,128)} all-gather(f32[3,16,1,128]{3,1,2,0:T(8,128)S(1)} %get-tuple-element.130), channel_id=7, replica_groups=mesh['lon'=32,'lat'=8] {'lon'}, dimensions={3}, use_global_device_ids=true | all-gather | bytes 811008 | tf_op jit(solution)/shard_map/all_gather | solution.py:76
  494.9 6.8 %copy.637 = f32[3,16,1,4096]{1,0,3,2:T(4,128)} copy(f32[3,16,1,4096]{3,1,2,0:T(8,128)} %all-gather.5) | data formatting | bytes 1572864 | tf_op jit(solution)/shard_map/all_gather | solution.py:76
  501.7 4.9 gather_fusion.6
  513.0 6.4 collective-permute-start.30
  521.3 47.6 %all-gather.6 = f32[3,16,1,4096]{3,1,2,0:T(8,128)S(1)} all-gather(f32[3,16,1,128]{3,1,2,0:T(8,128)S(1)} %get-tuple-element.120), channel_id=8, replica_groups=mesh['lon'=32,'lat'=8] {'lon'}, dimensions={3}, use_global_device_ids=true | all-gather | bytes 811008 | tf_op jit(solution)/shard_map/all_gather | solution.py:76
  568.9 5.8 copy.651
  574.7 4.3 gather_fusion.7
  583.9 85.9 %psum.7 = f32[]{:T(128)} all-reduce(f32[]{:T(128)} %get-tuple-element.93), channel_id=1, replica_groups=mesh['lon'=32,'lat'=8] {'lon','lat'}, use_global_device_ids=true, to_apply=%region_1.3 | all-reduce | flops 1 | bytes 8 | tf_op jit(solution)/shard_map/psum | solution.py:142
  (237 shorter events, 93.8 us)
Async XLA Ops:
  3.3 111.6 %collective-permute-start.6 = (f32[3,16,1,128]{3,1,0,2:T(8,128)}, f32[3,16,1,128]{3,1,0,2:T(8,128)}, u32[]{:S(2)}, u32[]{:S(2)}) collective-permute-start(f32[3,16,1,128]{3,1,0,2:T(8,128)} %get-tuple-element.160), channel_id=1, source_target_pairs={{0,1},{1,2},{2,3},{3,4},{4,5},{5,6},{6,7},{8,9},{9,10},{10,11},{11... | collective-permute-start | bytes 73736 | tf_op jit(solution)/shard_map/ppermute | solution.py:16
  7.9 106.9 %collective-permute-start.7 = (f32[3,16,1,128]{3,1,0,2:T(8,128)}, f32[3,16,1,128]{3,1,0,2:T(8,128)}, u32[]{:S(2)}, u32[]{:S(2)}) collective-permute-start(f32[3,16,1,128]{3,1,0,2:T(8,128)} %get-tuple-element.159), channel_id=1, source_target_pairs={{1,0},{2,1},{3,2},{4,3},{5,4},{6,5},{7,6},{9,8},{10,9},{11,10},{12... | collective-permute-start | bytes 73736 | tf_op jit(solution)/shard_map/ppermute | solution.py:19
  11.9 101.4 %collective-permute-start.5 = (f32[4,16,1,128]{3,2,1,0:T(1,128)}, f32[4,16,1,128]{3,2,1,0:T(1,128)}, u32[]{:S(2)}, u32[]{:S(2)}) collective-permute-start(f32[4,16,1,128]{3,2,1,0:T(1,128)} %get-tuple-element.119), channel_id=1, source_target_pairs={{1,0},{2,1},{3,2},{4,3},{5,4},{6,5},{7,6},{9,8},{10,9},{11,10},{12... | collective-permute-start | bytes 98312 | tf_op jit(solution)/shard_map/ppermute | solution.py:19
  15.9 100.2 %all-to-all-start = ((f32[32,3,16,128]{3,2,1,0:T(8,128)}), f32[32,3,16,128]{3,2,1,0:T(8,128)}, u32[]{:S(2)}, u32[]{:S(2)}) async-start(f32[32,3,16,128]{3,2,1,0:T(8,128)} %stack.17), calls=%async_computation | async-start | bytes 1572864 | tf_op jit(solution)/shard_map/all_to_all | solution.py:61
  29.1 71.6 %collective-permute-start.1 = (f32[4,16,16,1]{3,2,1,0:T(8,128)}, f32[4,16,16,1]{3,2,1,0:T(8,128)}, u32[]{:S(2)}, u32[]{:S(2)}) collective-permute-start(f32[4,16,16,1]{3,2,1,0:T(8,128)} %get-tuple-element.117), channel_id=1, source_target_pairs={{8,0},{16,8},{24,16},{32,24},{40,32},{48,40},{56,48},{64,56},{72,6... | collective-permute-start | bytes 12296 | tf_op jit(solution)/shard_map/ppermute | solution.py:19
  29.4 71.3 %collective-permute-start = (f32[4,16,16,1]{3,2,1,0:T(8,128)}, f32[4,16,16,1]{3,2,1,0:T(8,128)}, u32[]{:S(2)}, u32[]{:S(2)}) collective-permute-start(f32[4,16,16,1]{3,2,1,0:T(8,128)} %get-tuple-element.116), channel_id=1, source_target_pairs={{0,8},{8,16},{16,24},{24,32},{32,40},{40,48},{48,56},{56,64},{64,7... | collective-permute-start | bytes 12296 | tf_op jit(solution)/shard_map/ppermute | solution.py:16
  100.7 9.9 %collective-permute-start.3 = (f32[3,16,16,1]{3,2,1,0:T(8,128)}, f32[3,16,16,1]{3,2,1,0:T(8,128)S(1)}, u32[]{:S(2)}, u32[]{:S(2)}) collective-permute-start(f32[3,16,16,1]{3,2,1,0:T(8,128)} %get-tuple-element.156), channel_id=1, source_target_pairs={{8,0},{16,8},{24,16},{32,24},{40,32},{48,40},{56,48},{64,56},{72,6... | collective-permute-start | bytes 9224 | tf_op jit(solution)/shard_map/ppermute | solution.py:19
  105.8 7.6 %collective-permute-start.4 = (f32[4,16,1,128]{3,2,1,0:T(1,128)}, f32[4,16,1,128]{3,2,1,0:T(1,128)S(1)}, u32[]{:S(2)}, u32[]{:S(2)}) collective-permute-start(f32[4,16,1,128]{3,2,1,0:T(1,128)} %get-tuple-element.118), channel_id=1, source_target_pairs={{0,1},{1,2},{2,3},{3,4},{4,5},{5,6},{6,7},{8,9},{9,10},{10,11},{11... | collective-permute-start | bytes 98312 | tf_op jit(solution)/shard_map/ppermute | solution.py:16
  132.0 68.0 %collective-permute-start.10 = (f32[3,16,1,128]{3,1,0,2:T(8,128)S(1)}, f32[3,16,1,128]{3,1,0,2:T(8,128)S(1)}, u32[]{:S(2)}, u32[]{:S(2)}) collective-permute-start(f32[3,16,1,128]{3,1,0,2:T(8,128)S(1)} %get-tuple-element.155), channel_id=1, source_target_pairs={{0,1},{1,2},{2,3},{3,4},{4,5},{5,6},{6,7},{8,9},{9,10},{10,11},{11... | collective-permute-start | bytes 73736 | tf_op jit(solution)/shard_map/ppermute | solution.py:16
  135.7 64.3 %collective-permute-start.11 = (f32[3,16,1,128]{3,1,0,2:T(8,128)S(1)}, f32[3,16,1,128]{3,1,0,2:T(8,128)S(1)}, u32[]{:S(2)}, u32[]{:S(2)}) collective-permute-start(f32[3,16,1,128]{3,1,0,2:T(8,128)S(1)} %get-tuple-element.154), channel_id=1, source_target_pairs={{1,0},{2,1},{3,2},{4,3},{5,4},{6,5},{7,6},{9,8},{10,9},{11,10},{12... | collective-permute-start | bytes 73736 | tf_op jit(solution)/shard_map/ppermute | solution.py:19
  184.7 13.7 %collective-permute-start.8 = (f32[3,16,16,1]{3,2,1,0:T(8,128)}, f32[3,16,16,1]{3,2,1,0:T(8,128)}, u32[]{:S(2)}, u32[]{:S(2)}) collective-permute-start(f32[3,16,16,1]{3,2,1,0:T(8,128)} %get-tuple-element.152), channel_id=1, source_target_pairs={{0,8},{8,16},{16,24},{24,32},{32,40},{40,48},{48,56},{56,64},{64,7... | collective-permute-start | bytes 9224 | tf_op jit(solution)/shard_map/ppermute | solution.py:16
  186.5 11.9 %collective-permute-start.9 = (f32[3,16,16,1]{3,2,1,0:T(8,128)}, f32[3,16,16,1]{3,2,1,0:T(8,128)}, u32[]{:S(2)}, u32[]{:S(2)}) collective-permute-start(f32[3,16,16,1]{3,2,1,0:T(8,128)} %get-tuple-element.151), channel_id=1, source_target_pairs={{8,0},{16,8},{24,16},{32,24},{40,32},{48,40},{56,48},{64,56},{72,6... | collective-permute-start | bytes 9224 | tf_op jit(solution)/shard_map/ppermute | solution.py:19
  204.9 75.5 %collective-permute-start.14 = (f32[3,16,1,128]{3,1,0,2:T(8,128)S(1)}, f32[3,16,1,128]{3,1,0,2:T(8,128)S(1)}, u32[]{:S(2)}, u32[]{:S(2)}) collective-permute-start(f32[3,16,1,128]{3,1,0,2:T(8,128)S(1)} %get-tuple-element.150), channel_id=1, source_target_pairs={{0,1},{1,2},{2,3},{3,4},{4,5},{5,6},{6,7},{8,9},{9,10},{10,11},{11... | collective-permute-start | bytes 73736 | tf_op jit(solution)/shard_map/ppermute | solution.py:16
  209.2 71.2 %collective-permute-start.15 = (f32[3,16,1,128]{3,1,0,2:T(8,128)S(1)}, f32[3,16,1,128]{3,1,0,2:T(8,128)S(1)}, u32[]{:S(2)}, u32[]{:S(2)}) collective-permute-start(f32[3,16,1,128]{3,1,0,2:T(8,128)S(1)} %get-tuple-element.149), channel_id=1, source_target_pairs={{1,0},{2,1},{3,2},{4,3},{5,4},{6,5},{7,6},{9,8},{10,9},{11,10},{12... | collective-permute-start | bytes 73736 | tf_op jit(solution)/shard_map/ppermute | solution.py:19
  210.5 67.2 %collective-permute-start.12 = (f32[3,16,16,1]{3,1,0,2:T(8,128)}, f32[3,16,16,1]{3,1,0,2:T(8,128)}, u32[]{:S(2)}, u32[]{:S(2)}) collective-permute-start(f32[3,16,16,1]{3,1,0,2:T(8,128)} %get-tuple-element.147), channel_id=1, source_target_pairs={{0,8},{8,16},{16,24},{24,32},{32,40},{40,48},{48,56},{56,64},{64,7... | collective-permute-start | bytes 9224 | tf_op jit(solution)/shard_map/ppermute | solution.py:16
  212.6 66.2 %collective-permute-start.13 = (f32[3,16,16,1]{3,1,0,2:T(8,128)}, f32[3,16,16,1]{3,1,0,2:T(8,128)}, u32[]{:S(2)}, u32[]{:S(2)}) collective-permute-start(f32[3,16,16,1]{3,1,0,2:T(8,128)} %get-tuple-element.146), channel_id=1, source_target_pairs={{8,0},{16,8},{24,16},{32,24},{40,32},{48,40},{56,48},{64,56},{72,6... | collective-permute-start | bytes 9224 | tf_op jit(solution)/shard_map/ppermute | solution.py:19
  285.1 72.5 %collective-permute-start.18 = (f32[3,16,1,128]{3,1,0,2:T(8,128)S(1)}, f32[3,16,1,128]{3,1,0,2:T(8,128)}, u32[]{:S(2)}, u32[]{:S(2)}) collective-permute-start(f32[3,16,1,128]{3,1,0,2:T(8,128)S(1)} %get-tuple-element.145), channel_id=1, source_target_pairs={{0,1},{1,2},{2,3},{3,4},{4,5},{5,6},{6,7},{8,9},{9,10},{10,11},{11... | collective-permute-start | bytes 73736 | tf_op jit(solution)/shard_map/ppermute | solution.py:16
  289.9 67.7 %collective-permute-start.19 = (f32[3,16,1,128]{3,1,0,2:T(8,128)S(1)}, f32[3,16,1,128]{3,1,0,2:T(8,128)}, u32[]{:S(2)}, u32[]{:S(2)}) collective-permute-start(f32[3,16,1,128]{3,1,0,2:T(8,128)S(1)} %get-tuple-element.144), channel_id=1, source_target_pairs={{1,0},{2,1},{3,2},{4,3},{5,4},{6,5},{7,6},{9,8},{10,9},{11,10},{12... | collective-permute-start | bytes 73736 | tf_op jit(solution)/shard_map/ppermute | solution.py:19
  291.2 63.6 %collective-permute-start.16 = (f32[3,16,16,1]{3,1,0,2:T(8,128)}, f32[3,16,16,1]{3,1,0,2:T(8,128)}, u32[]{:S(2)}, u32[]{:S(2)}) collective-permute-start(f32[3,16,16,1]{3,1,0,2:T(8,128)} %get-tuple-element.142), channel_id=1, source_target_pairs={{0,8},{8,16},{16,24},{24,32},{32,40},{40,48},{48,56},{56,64},{64,7... | collective-permute-start | bytes 9224 | tf_op jit(solution)/shard_map/ppermute | solution.py:16
  291.3 64.7 %collective-permute-start.17 = (f32[3,16,16,1]{3,1,0,2:T(8,128)}, f32[3,16,16,1]{3,1,0,2:T(8,128)}, u32[]{:S(2)}, u32[]{:S(2)}) collective-permute-start(f32[3,16,16,1]{3,1,0,2:T(8,128)} %get-tuple-element.141), channel_id=1, source_target_pairs={{8,0},{16,8},{24,16},{32,24},{40,32},{48,40},{56,48},{64,56},{72,6... | collective-permute-start | bytes 9224 | tf_op jit(solution)/shard_map/ppermute | solution.py:19
  361.6 71.5 %collective-permute-start.22 = (f32[3,16,1,128]{3,1,0,2:T(8,128)S(1)}, f32[3,16,1,128]{3,1,0,2:T(8,128)S(1)}, u32[]{:S(2)}, u32[]{:S(2)}) collective-permute-start(f32[3,16,1,128]{3,1,0,2:T(8,128)S(1)} %get-tuple-element.138), channel_id=1, source_target_pairs={{0,1},{1,2},{2,3},{3,4},{4,5},{5,6},{6,7},{8,9},{9,10},{10,11},{11... | collective-permute-start | bytes 73736 | tf_op jit(solution)/shard_map/ppermute | solution.py:16
  366.7 66.4 %collective-permute-start.23 = (f32[3,16,1,128]{3,2,1,0:T(1,128)S(1)}, f32[3,16,1,128]{3,2,1,0:T(1,128)S(1)}, u32[]{:S(2)}, u32[]{:S(2)}) collective-permute-start(f32[3,16,1,128]{3,2,1,0:T(1,128)S(1)} %slice.756), channel_id=1, source_target_pairs={{1,0},{2,1},{3,2},{4,3},{5,4},{6,5},{7,6},{9,8},{10,9},{11,10},{12... | collective-permute-start | bytes 73736 | tf_op jit(solution)/shard_map/ppermute | solution.py:19
  368.0 63.5 %collective-permute-start.20 = (f32[3,16,16,1]{3,1,0,2:T(8,128)S(1)}, f32[3,16,16,1]{3,1,0,2:T(8,128)}, u32[]{:S(2)}, u32[]{:S(2)}) collective-permute-start(f32[3,16,16,1]{3,1,0,2:T(8,128)S(1)} %get-tuple-element.140), channel_id=1, source_target_pairs={{0,8},{8,16},{16,24},{24,32},{32,40},{40,48},{48,56},{56,64},{64,7... | collective-permute-start | bytes 9224 | tf_op jit(solution)/shard_map/ppermute | solution.py:16
  368.1 63.4 %collective-permute-start.21 = (f32[3,16,16,1]{3,1,0,2:T(8,128)S(1)}, f32[3,16,16,1]{3,1,0,2:T(8,128)}, u32[]{:S(2)}, u32[]{:S(2)}) collective-permute-start(f32[3,16,16,1]{3,1,0,2:T(8,128)S(1)} %get-tuple-element.139), channel_id=1, source_target_pairs={{8,0},{16,8},{24,16},{32,24},{40,32},{48,40},{56,48},{64,56},{72,6... | collective-permute-start | bytes 9224 | tf_op jit(solution)/shard_map/ppermute | solution.py:19
  436.6 72.6 %collective-permute-start.26 = (f32[3,16,1,128]{3,1,0,2:T(8,128)S(1)}, f32[3,16,1,128]{3,1,0,2:T(8,128)S(1)}, u32[]{:S(2)}, u32[]{:S(2)}) collective-permute-start(f32[3,16,1,128]{3,1,0,2:T(8,128)S(1)} %get-tuple-element.131), channel_id=1, source_target_pairs={{0,1},{1,2},{2,3},{3,4},{4,5},{5,6},{6,7},{8,9},{9,10},{10,11},{11... | collective-permute-start | bytes 73736 | tf_op jit(solution)/shard_map/ppermute | solution.py:16
  443.0 66.2 %collective-permute-start.27 = (f32[3,16,1,128]{3,1,0,2:T(8,128)S(1)}, f32[3,16,1,128]{3,1,0,2:T(8,128)S(1)}, u32[]{:S(2)}, u32[]{:S(2)}) collective-permute-start(f32[3,16,1,128]{3,1,0,2:T(8,128)S(1)} %get-tuple-element.132), channel_id=1, source_target_pairs={{1,0},{2,1},{3,2},{4,3},{5,4},{6,5},{7,6},{9,8},{10,9},{11,10},{12... | collective-permute-start | bytes 73736 | tf_op jit(solution)/shard_map/ppermute | solution.py:19
  444.3 63.5 %collective-permute-start.24 = (f32[3,16,16,1]{3,1,0,2:T(8,128)S(1)}, f32[3,16,16,1]{3,1,0,2:T(8,128)}, u32[]{:S(2)}, u32[]{:S(2)}) collective-permute-start(f32[3,16,16,1]{3,1,0,2:T(8,128)S(1)} %get-tuple-element.134), channel_id=1, source_target_pairs={{0,8},{8,16},{16,24},{24,32},{32,40},{40,48},{48,56},{56,64},{64,7... | collective-permute-start | bytes 9224 | tf_op jit(solution)/shard_map/ppermute | solution.py:16
  444.3 63.4 %collective-permute-start.25 = (f32[3,16,16,1]{3,1,0,2:T(8,128)S(1)}, f32[3,16,16,1]{3,1,0,2:T(8,128)}, u32[]{:S(2)}, u32[]{:S(2)}) collective-permute-start(f32[3,16,16,1]{3,1,0,2:T(8,128)S(1)} %get-tuple-element.133), channel_id=1, source_target_pairs={{8,0},{16,8},{24,16},{32,24},{40,32},{48,40},{56,48},{64,56},{72,6... | collective-permute-start | bytes 9224 | tf_op jit(solution)/shard_map/ppermute | solution.py:19
  513.0 67.5 %collective-permute-start.30 = (f32[3,16,1,128]{3,1,0,2:T(8,128)S(1)}, f32[3,16,1,128]{3,1,0,2:T(8,128)S(1)}, u32[]{:S(2)}, u32[]{:S(2)}) collective-permute-start(f32[3,16,1,128]{3,1,0,2:T(8,128)S(1)} %get-tuple-element.121), channel_id=1, source_target_pairs={{0,1},{1,2},{2,3},{3,4},{4,5},{5,6},{6,7},{8,9},{9,10},{10,11},{11... | collective-permute-start | bytes 73736 | tf_op jit(solution)/shard_map/ppermute | solution.py:16
  519.4 61.1 %collective-permute-start.31 = (f32[3,16,1,128]{3,1,0,2:T(8,128)S(1)}, f32[3,16,1,128]{3,1,0,2:T(8,128)S(1)}, u32[]{:S(2)}, u32[]{:S(2)}) collective-permute-start(f32[3,16,1,128]{3,1,0,2:T(8,128)S(1)} %get-tuple-element.122), channel_id=1, source_target_pairs={{1,0},{2,1},{3,2},{4,3},{5,4},{6,5},{7,6},{9,8},{10,9},{11,10},{12... | collective-permute-start | bytes 73736 | tf_op jit(solution)/shard_map/ppermute | solution.py:19
  520.7 58.4 %collective-permute-start.28 = (f32[3,16,16,1]{3,1,0,2:T(8,128)}, f32[3,16,16,1]{3,1,0,2:T(8,128)}, u32[]{:S(2)}, u32[]{:S(2)}) collective-permute-start(f32[3,16,16,1]{3,1,0,2:T(8,128)} %get-tuple-element.124), channel_id=1, source_target_pairs={{0,8},{8,16},{16,24},{24,32},{32,40},{40,48},{48,56},{56,64},{64,7... | collective-permute-start | bytes 9224 | tf_op jit(solution)/shard_map/ppermute | solution.py:16
  520.8 58.3 %collective-permute-start.29 = (f32[3,16,16,1]{3,1,0,2:T(8,128)}, f32[3,16,16,1]{3,1,0,2:T(8,128)}, u32[]{:S(2)}, u32[]{:S(2)}) collective-permute-start(f32[3,16,16,1]{3,1,0,2:T(8,128)} %get-tuple-element.123), channel_id=1, source_target_pairs={{8,0},{16,8},{24,16},{32,24},{40,32},{48,40},{56,48},{64,56},{72,6... | collective-permute-start | bytes 9224 | tf_op jit(solution)/shard_map/ppermute | solution.py:19
  (34 other events, 1661.4 us)
